TPU v7x, 32 devices: a whole 2x2x4 slice. The times are simulated.
32 devices in a mesh: req: 2 (over x), seq: 16 (over z, y, core).
Axes of the slice: x: 2, y: 2, z: 4, core: 2. Of those that a mesh axis runs over, the one named last changes fastest.
Arguments:
- states: bfloat16 [4, 4, 4544], P(None, 'req', 'seq'), may hold values from -6 to 6
- kv_cache: bfloat16 [4, 8192, 128], P('req', 'seq'), may hold values from -48 to 48, as said below
- lengths: int32 [4], replicated, may hold values from 1 to 8188, as said below
- placement: int32 [4], replicated, may hold values from 0 to 3, each once
- norm_gain: bfloat16 [4544], replicated, may hold values from 0.25 to 1.75
- norm_bias: bfloat16 [4544], replicated, may hold values from -1.5 to 1.5
- w_query: bfloat16 [4544, 4544], P('req', 'seq'), may hold values from -0.09375 to 0.09375
- w_keyval: bfloat16 [4544, 128], P('req'), may hold values from -0.09375 to 0.09375
- w_out: bfloat16 [4544, 4544], P('seq', 'req'), may hold values from -0.09375 to 0.09375
- w_up: bfloat16 [4544, 18176], P('req', 'seq'), may hold values from -0.09375 to 0.09375
- w_down: bfloat16 [18176, 4544], P('seq', 'req'), may hold values from -0.046875 to 0.046875
Outputs:
- new_states: bfloat16 [4, 4, 4544], P(None, 'req', 'seq')
- new_cache: bfloat16 [4, 8192, 128], P('req', 'seq')
Inputs may be any that keep to these rules, and one draw needn't show every extreme that they name: Request r's cache holds its first lengths[r] positions; some request has exactly 8188. `kv_cache`: row i is the cache of request placement[i]; positions at or beyond that request's length hold arbitrary values. `placement`: each request is served by exactly one slot.
All inputs are finite; a program needn't handle non-finite values.
Results may differ from a plain program's by a relative error of at most 0.012.
The roundings to bfloat16 on the way count: a program that leaves them out, or rounds other values in their place, can miss the bound.
Values may be sent and summed in bfloat16 or wider, within the bound.
No kernel may reach another device: no remote copies, remote signals or barrier semaphores. Data moves between devices by JAX's collectives and lax.ppermute only.
A program may use at most 192 MiB of HBM per device.

v0:
```python
import jax
import jax.numpy as jnp
from jax import lax
from jax.sharding import PartitionSpec as P

EPSILON = 1e-05
NEGATIVE = -1e30
ALL = ("req", "seq")


def layer_norm(row_block, norm_gain, norm_bias):
    values = row_block.astype(jnp.float32)
    average = jnp.mean(values, axis=-1, keepdims=True)
    centered = values - average
    spread = jnp.mean(centered * centered, axis=-1, keepdims=True)
    scaled = centered * lax.rsqrt(spread + EPSILON)
    return (scaled * norm_gain.astype(jnp.float32) + norm_bias.astype(jnp.float32)).astype(
        jnp.bfloat16
    )


def rotate(vectors, positions):
    head_width = vectors.shape[-1]
    half_width = head_width // 2
    frequency = 10000.0 ** (-(jnp.arange(half_width, dtype=jnp.float32) * 2.0) / head_width)
    angles = positions.astype(jnp.float32)[:, None] * frequency[None, :]
    cosine = jnp.concatenate([jnp.cos(angles), jnp.cos(angles)], axis=-1)[:, None, :]
    sine_wave = jnp.concatenate([jnp.sin(angles), jnp.sin(angles)], axis=-1)[:, None, :]
    turned = jnp.concatenate([-vectors[..., half_width:], vectors[..., :half_width]], axis=-1)
    return vectors * cosine + turned * sine_wave


def shards(
    states,
    kv_cache,
    lengths,
    placement,
    norm_gain,
    norm_bias,
    w_query,
    w_keyval,
    w_out,
    w_up,
    w_down,
):
    steps = states.shape[0]
    group_rows = kv_cache.shape[0]
    seg_length = kv_cache.shape[1]
    head_width = kv_cache.shape[2] // 2
    model_width = norm_gain.shape[0]
    head_count = model_width // head_width
    slice_width = states.shape[2]
    part_width = w_query.shape[0]
    total = placement.shape[0]
    req_size = total // group_rows
    seq_size = model_width // slice_width
    rows = steps * total
    group_index = lax.axis_index("req")
    shard_index = lax.axis_index("seq")
    own_requests = lax.dynamic_slice_in_dim(placement, group_index * group_rows, group_rows, 0)
    slot_lengths = jnp.take(lengths, own_requests)
    step_offsets = jnp.arange(steps, dtype=jnp.int32)
    positions = slot_lengths[None, :] + step_offsets[:, None]
    every = lax.all_gather(states, ALL, axis=0, tiled=False)
    every = every.reshape(req_size, seq_size, steps, group_rows, slice_width)
    every = every.transpose(2, 0, 3, 1, 4).reshape(steps, total, model_width)
    current_all = jnp.take(every, placement, axis=1)
    normed = layer_norm(current_all.reshape(rows, model_width), norm_gain, norm_bias)
    normed_part = lax.dynamic_slice_in_dim(normed, group_index * part_width, part_width, 1)
    part_query = jnp.dot(normed_part, w_query, preferred_element_type=jnp.float32)
    part_keyval = jnp.dot(normed_part, w_keyval, preferred_element_type=jnp.float32)
    part_up = jnp.dot(normed_part, w_up, preferred_element_type=jnp.float32)
    first = lax.psum(jnp.concatenate([part_query, part_keyval, part_up], axis=1), "req")
    query_raw = first[:, :slice_width].astype(jnp.bfloat16).reshape(steps, total, slice_width)
    keyval = first[:, slice_width : slice_width + 2 * head_width].reshape(
        steps, total, 2 * head_width
    )
    up_part = first[:, slice_width + 2 * head_width :]
    own_query = lax.dynamic_slice_in_dim(query_raw, group_index * group_rows, group_rows, 1)
    query_all = lax.all_gather(own_query, "seq", axis=2, tiled=True)
    flat_positions = positions.reshape(-1)
    query_rows = rotate(
        query_all.astype(jnp.float32).reshape(steps * group_rows, head_count, head_width),
        flat_positions,
    ).astype(jnp.bfloat16)
    own_keyval = lax.dynamic_slice_in_dim(keyval, group_index * group_rows, group_rows, 1)
    own_keyval = own_keyval.reshape(steps * group_rows, 2 * head_width)
    new_key = rotate(own_keyval[:, None, :head_width], flat_positions)[:, 0, :]
    new_entry = jnp.concatenate([new_key, own_keyval[:, head_width:]], axis=-1).astype(jnp.bfloat16)
    new_entry = new_entry.reshape(steps, group_rows, 2 * head_width)
    local_slots = jnp.arange(seg_length, dtype=jnp.int32)
    global_positions = shard_index * seg_length + local_slots
    cache_now = kv_cache
    for step_index in range(steps):
        write_mask = global_positions[None, :] == positions[step_index][:, None]
        cache_now = jnp.where(write_mask[:, :, None], new_entry[step_index][:, None, :], cache_now)
    key_rows = cache_now[:, :, :head_width]
    value_rows = cache_now[:, :, head_width:]
    query_heads = (
        query_rows.reshape(steps, group_rows, head_count, head_width)
        .transpose(1, 0, 2, 3)
        .reshape(group_rows, steps * head_count, head_width)
    )
    scores = jnp.einsum(
        "gqd,gsd->gqs", query_heads, key_rows, preferred_element_type=jnp.float32
    ) * head_width ** (-0.5)
    valid = global_positions[None, None, :] <= positions.T[:, :, None]
    valid = jnp.broadcast_to(
        valid[:, :, None, :], (group_rows, steps, head_count, seg_length)
    ).reshape(group_rows, steps * head_count, seg_length)
    local_peak = jnp.max(jnp.where(valid, scores, NEGATIVE), axis=-1)
    weights = jnp.where(valid, jnp.exp(scores - local_peak[:, :, None]), 0.0)
    local_total = jnp.sum(weights, axis=-1)
    local_weighted = jnp.einsum(
        "gqs,gsd->gqd", weights, value_rows, preferred_element_type=jnp.float32
    )
    peak_buffer = jnp.full((total, steps * head_count), NEGATIVE, jnp.float32)
    peak_buffer = lax.dynamic_update_slice_in_dim(
        peak_buffer, local_peak, group_index * group_rows, 0
    )
    peak = lax.pmax(peak_buffer, ALL)
    own_peak = lax.dynamic_slice_in_dim(peak, group_index * group_rows, group_rows, 0)
    scale = jnp.exp(local_peak - own_peak)
    packed = jnp.concatenate(
        [local_weighted * scale[:, :, None], (local_total * scale)[:, :, None]], axis=-1
    )
    packed_buffer = jnp.zeros((total, steps * head_count, head_width + 1), jnp.float32)
    packed_buffer = lax.dynamic_update_slice_in_dim(
        packed_buffer, packed, group_index * group_rows, 0
    )
    summed = lax.psum(packed_buffer, ALL)
    mixed = summed[:, :, :head_width] / summed[:, :, head_width:]
    mixed = (
        mixed.reshape(total, steps, model_width)
        .transpose(1, 0, 2)
        .reshape(rows, model_width)
        .astype(jnp.bfloat16)
    )
    mixed_part = lax.dynamic_slice_in_dim(mixed, shard_index * slice_width, slice_width, 1)
    hidden = jax.nn.gelu(up_part, approximate=False).astype(jnp.bfloat16)
    partial_sum = jnp.dot(mixed_part, w_out, preferred_element_type=jnp.float32) + jnp.dot(
        hidden, w_down, preferred_element_type=jnp.float32
    )
    out_buffer = jnp.zeros((rows, model_width), jnp.float32)
    out_buffer = lax.dynamic_update_slice_in_dim(
        out_buffer, partial_sum, group_index * part_width, 1
    )
    branch = lax.psum(out_buffer, ALL).reshape(steps, total, model_width)
    inverse = jnp.zeros((total,), jnp.int32).at[placement].set(jnp.arange(total, dtype=jnp.int32))
    own_inverse = lax.dynamic_slice_in_dim(inverse, group_index * group_rows, group_rows, 0)
    own_branch = jnp.take(branch, own_inverse, axis=1)
    own_branch = lax.dynamic_slice_in_dim(own_branch, shard_index * slice_width, slice_width, 2)
    new_states = (states.astype(jnp.float32) + own_branch).astype(jnp.bfloat16)
    return (new_states, cache_now)


def solution(mesh):
    in_specs = (
        P(None, "req", "seq"),
        P("req", "seq", None),
        P(),
        P(),
        P(),
        P(),
        P("req", "seq"),
        P("req", None),
        P("seq", "req"),
        P("req", "seq"),
        P("seq", "req"),
    )
    out_specs = (P(None, "req", "seq"), P("req", "seq", None))
    return jax.shard_map(shards, mesh=mesh, in_specs=in_specs, out_specs=out_specs, check_vma=False)
```

profile of v0, /device:TPU:8, one launch (start us, length us, event | category | flops | bytes accessed | tf_op | source)
XLA Modules:
  0.0 437.4 jit_solution(13402356280962080718)
XLA Ops:
  7.2 0.8 compare_select_fusion.2
  8.0 0.7 compare_and_fusion
  8.6 0.8 dynamic-slice.1
  9.4 0.8 dynamic-slice.2
  10.2 38.8 %all-gather = bf16[128,2,284]{2,1,0:T(2,128)(2,1)S(1)} all-gather(bf16[4,2,284]{2,1,0:T(2,128)(2,1)} %param.11), channel_id=2, replica_groups=mesh['req'=2,'seq'=16] {'req','seq'}, dimensions={0}, use_global_device_ids=true | all-gather | bytes 149952 | tf_op jit(solution)/shard_map/all_gather | solution.py:64
  49.0 0.3 reshape.348
  49.4 0.7 gather_fusion.1
  50.1 0.3 convert_reduce_fusion
  50.4 0.3 fusion.5
  51.3 3.5 fusion.96
  54.8 0.3 fusion.94
  55.1 0.4 fusion.95
  55.5 0.8 concatenate.40
  56.5 0.6 gather_fusion
  57.7 0.1 copy.81
  58.0 0.2 reshape.346
  58.3 19.3 %all-reduce.4.cloned.1.call-done = f32[16,1548]{1,0:T(8,128)} async-done(((f32[16,1548]{1,0:T(8,128)}), f32[16,1548]{1,0:T(8,128)}) %all-reduce.4.cloned.1.call-update) | async-done | bytes 99088 | tf_op jit(solution)/shard_map/psum | solution.py:73
  77.6 0.8 slice.99
  78.4 0.7 slice.124
  79.2 0.2 copy.88
  79.4 32.2 %all_gather.11 = bf16[4,2,4544]{0,1,2:T(2,128)(2,1)} all-gather(bf16[4,2,284]{0,1,2:T(2,128)(2,1)S(1)} %copy.88), channel_id=1, replica_groups=mesh['req'=2,'seq'=16] {'seq'}, dimensions={2}, use_global_device_ids=true | all-gather | bytes 77248 | tf_op jit(solution)/shard_map/all_gather | solution.py:80
  111.6 5.2 %copy.73 = bf16[4,2,4544]{2,0,1:T(4,128)(2,1)S(1)} copy(bf16[4,2,4544]{0,1,2:T(2,128)(2,1)} %all_gather.11) | data formatting | bytes 145408 | tf_op jit(solution)/shard_map/all_gather | solution.py:80
  116.8 0.2 reshape.351
  117.1 0.2 reshape.350
  117.9 0.2 copy.78
  118.1 0.2 fusion.8
  118.2 0.2 copy.80
  118.5 0.2 select_select_fusion
  118.8 0.5 select_reduce_fusion
  119.3 41.3 %pmax.7 = f32[4,284]{1,0:T(4,128)S(1)} all-reduce(f32[4,284]{1,0:T(4,128)S(1)} %constant_dynamic-update-slice_fusion.1), channel_id=1, replica_groups=mesh['req'=2,'seq'=16] {'req','seq'}, use_global_device_ids=true, to_apply=%region_5.6 | all-reduce | flops 1136 | bytes 9088 | tf_op jit(solution)/shard_map/pmax | solution.py:121
  160.6 0.4 fusion
  161.0 0.4 convolution_multiply_fusion.1
  161.5 0.2 copy.82
  161.7 0.8 copy-done.2
  162.6 0.6 scatter_custom_fusion
  163.2 129.3 %all-reduce.6.cloned.1.call-done = f32[4,284,65]{2,1,0:T(8,128)} async-done(((f32[4,284,65]{2,1,0:T(8,128)}), f32[4,284,65]{2,1,0:T(8,128)}) %all-reduce.6.cloned.1.call-update) | async-done | bytes 295376 | tf_op jit(solution)/shard_map/psum | solution.py:131
  292.5 1.5 slice_reduce_fusion
  294.0 1.3 fusion.1
  295.3 0.2 convert_element_type.69
  295.6 0.4 fusion.55
  296.0 0.2 copy-done.6
  296.2 3.4 convolution_add_fusion
  299.7 1.3 dynamic_update_slice.11
  301.1 0.8 copy.84
  302.0 0.8 copy.86
  302.9 125.7 %all-reduce.8.cloned.1.call-done = f32[4,4,4544]{2,0,1:T(4,128)} async-done(((f32[4,4,4544]{2,0,1:T(4,128)}), f32[4,4,4544]{2,0,1:T(4,128)}) %all-reduce.8.cloned.1.call-update) | async-done | bytes 290832 | tf_op jit(solution)/shard_map/psum | solution.py:148
  428.5 1.6 gather_fusion.2
  430.2 0.6 copy.85
  (81 shorter events, 3.2 us)
Async XLA Ops:
  7.2 288.4 %copy-start = (bf16[284,2272]{1,0:T(8,128)(2,1)S(1)}, bf16[284,2272]{1,0:T(8,128)(2,1)}, u32[]{:S(2)}) copy-start(bf16[284,2272]{1,0:T(8,128)(2,1)} %param.19) | copy-start | bytes 3871492
  7.2 70.4 %all-reduce.4.cloned.1.call-start = ((), (), s32[]{:S(2)}) async-start(), calls=%async_computation | async-start | bytes 212992 | tf_op jit(solution)/shard_map/psum | solution.py:73
  51.3 3.5 copy-start.4
  51.3 3.8 copy-start.3
  54.8 1.6 copy-start.8
  54.8 1.7 copy-start.1
  55.1 2.6 copy-start.5
  56.3 236.2 %all-reduce.6.cloned.1.call-start = ((), (), s32[]{:S(2)}) async-start(), calls=%async_computation.1 | async-start | bytes 1179648 | tf_op jit(solution)/shard_map/psum | solution.py:131
  161.7 0.8 copy-start.2
  162.6 266.0 %all-reduce.8.cloned.1.call-start = ((), (), s32[]{:S(2)}) async-start(), calls=%async_computation.2 | async-start | bytes 589824 | tf_op jit(solution)/shard_map/psum | solution.py:148
  295.3 0.9 copy-start.6
  301.0 129.2 %copy-start.7 = (bf16[4,2,284]{2,1,0:T(2,128)(2,1)S(1)}, bf16[4,2,284]{2,1,0:T(2,128)(2,1)}, u32[]{:S(2)}) copy-start(bf16[4,2,284]{2,1,0:T(2,128)(2,1)} %param.11) | copy-start | bytes 13636
Sparse Core Ops, SparseCore 0:
  56.4 21.1 all-reduce.3
  162.7 129.7 all-reduce.5
  302.1 126.4 all-reduce.7
where the time goes:
time: 438 us; the launch traced here: 437 us
  waiting for transfers between devices  274 us (63%)
  blocking collectives  112 us (26%)
  local copies, waits for them, and re-layouts  22.3 us (5%)
  between operations  14.2 us (3%)
  matrix products  8.89 us (2%)
  other arithmetic  5.32 us (1%)
    psum x1, waiting for transfers between devices, shards(): summed = lax.psum(packed_buffer, ALL)  129 us
    psum x1, waiting for transfers between devices, shards(): branch = lax.psum(out_buffer, ALL).reshape(steps, total, model_width)  126 us
    pmax x1, blocking collectives, shards(): peak = lax.pmax(peak_buffer, ALL)  41.3 us
    all_gather x1, blocking collectives, shards(): every = lax.all_gather(states, ALL, axis=0, tiled=False)  38.8 us
    all_gather x1, blocking collectives, shards(): query_all = lax.all_gather(own_query, 'seq', axis=2, tiled=True)  32.2 us
    psum x1, waiting for transfers between devices, shards(): lax.psum(jnp.concatenate([part_query, part_keyval, part_up], axis=1), 'req')  19.3 us
  transfers between devices with their start and end apart: 3, of which 3 were waited for; matrix products, arithmetic and copies ran while one was open for 1% of the time, Pallas kernels for 0%

commit v1 on v0

--- a/solution.py
+++ b/solution.py
@@ -77,7 +77,21 @@
     )
     up_part = first[:, slice_width + 2 * head_width :]
     own_query = lax.dynamic_slice_in_dim(query_raw, group_index * group_rows, group_rows, 1)
-    query_all = lax.all_gather(own_query, "seq", axis=2, tiled=True)
+    how_many = lax.psum(1, "seq")
+    parts_seen = [(ii, (ii + 1) % how_many) for ii in range(how_many)]
+    u1, side_arr = ([own_query], [own_query])
+    fields = [(ii, (ii - 1) % how_many) for ii in range(how_many)]
+    for _ in range(how_many // 2):
+        u1.append(lax.ppermute(u1[-1], "seq", parts_seen))
+    at = 0
+    while at < (how_many - 1) // 2:
+        side_arr.append(lax.ppermute(side_arr[-1], "seq", perm=fields))
+        at += 1
+    query_all = jnp.roll(
+        jnp.concatenate([*u1[::-1], *side_arr[1:]], axis=2),
+        (lax.axis_index("seq") - how_many // 2) * own_query.shape[2],
+        axis=2,
+    )
     flat_positions = positions.reshape(-1)
     query_rows = rotate(
         query_all.astype(jnp.float32).reshape(steps * group_rows, head_count, head_width),

time: 438 us -> 441 us (level)
  blocking collectives: 112 us -> 91.6 us
  starting transfers between devices: 0.12 us -> 18.5 us
  waiting for transfers between devices: 274 us -> 285 us
  local copies, waits for them, and re-layouts: 22.3 us -> 16.8 us
    all_gather x1 -> x0, blocking collectives: 32.2 us -> none  [shards(): query_all = lax.all_gather(own_query, 'seq', axis=2, tiled=True)]
    ppermute x0 -> x15, starting transfers between devices: none -> 18.4 us  [the longest x7 18.3 us: shards(): side_arr.append(lax.ppermute(side_arr[-1], 'seq', perm=fields))]
    ppermute x0 -> x15, waiting for transfers between devices: none -> 12.1 us  [the longest x8 8.3 us: shards(): u1.append(lax.ppermute(u1[-1], 'seq', parts_seen))]
    pmax x1, blocking collectives: 41.3 us -> 52.7 us  [shards(): peak = lax.pmax(peak_buffer, ALL)]
    all_gather x1 -> x0, local copies, waits for them, and re-layouts: 5.18 us -> none  [shards(): query_all = lax.all_gather(own_query, 'seq', axis=2, tiled=True)]
  transfers between devices with their start and end apart: 3 -> 18, of which waited for: 3 -> 18; matrix products, arithmetic and copies ran while one was open for 1% -> 1% of each run, Pallas kernels for 0% -> 0%
where the time goes in v1:
time: 441 us; the launch traced here: 440 us
  waiting for transfers between devices  285 us (65%)
  blocking collectives  91.6 us (21%)
  starting transfers between devices  18.5 us (4%)
  local copies, waits for them, and re-layouts  16.8 us (4%)
  between operations  14.2 us (3%)
  matrix products  8.91 us (2%)
  other arithmetic  5.47 us (1%)
    psum x1, waiting for transfers between devices, shards(): summed = lax.psum(packed_buffer, ALL)  127 us
    psum x1, waiting for transfers between devices, shards(): branch = lax.psum(out_buffer, ALL).reshape(steps, total, model_width)  126 us
    pmax x1, blocking collectives, shards(): peak = lax.pmax(peak_buffer, ALL)  52.7 us
    all_gather x1, blocking collectives, shards(): every = lax.all_gather(states, ALL, axis=0, tiled=False)  38.8 us
    psum x1, waiting for transfers between devices, shards(): lax.psum(jnp.concatenate([part_query, part_keyval, part_up], axis=1), 'req')  19.8 us
    ppermute x7, starting transfers between devices, shards(): side_arr.append(lax.ppermute(side_arr[-1], 'seq', perm=fields))  18.3 us
  transfers between devices with their start and end apart: 18, of which 18 were waited for; matrix products, arithmetic and copies ran while one was open for 1% of the time, Pallas kernels for 0%

profile of v1, /device:TPU:8, one launch (start us, length us, event | category | flops | bytes accessed | tf_op | source)
XLA Modules:
  0.0 440.2 jit_solution(4003512747628434265)
XLA Ops:
  7.2 0.8 compare_select_fusion.2
  8.0 0.7 compare_and_fusion
  8.6 0.8 dynamic-slice.1
  9.4 0.8 dynamic-slice.2
  10.2 38.8 %all-gather = bf16[128,2,284]{2,1,0:T(2,128)(2,1)S(1)} all-gather(bf16[4,2,284]{2,1,0:T(2,128)(2,1)} %param.11), channel_id=2, replica_groups=mesh['req'=2,'seq'=16] {'req','seq'}, dimensions={0}, use_global_device_ids=true | all-gather | bytes 149952 | tf_op jit(solution)/shard_map/all_gather | solution.py:64
  49.4 0.7 gather_fusion.1
  51.3 3.5 fusion.96
  55.1 0.4 fusion.95
  55.5 0.8 concatenate.46
  56.5 0.6 gather_fusion
  57.8 19.8 %all-reduce.4.cloned.1.call-done = f32[16,1548]{1,0:T(8,128)} async-done(((f32[16,1548]{1,0:T(8,128)}), f32[16,1548]{1,0:T(8,128)}) %all-reduce.4.cloned.1.call-update) | async-done | bytes 99088 | tf_op jit(solution)/shard_map/psum | solution.py:73
  77.6 0.8 slice.124
  79.0 2.7 collective-permute-start.8
  81.8 0.6 collective-permute-done
  82.5 0.6 collective-permute-done.8
  83.1 2.6 collective-permute-start.9
  85.7 0.7 collective-permute-done.1
  86.4 0.6 collective-permute-done.9
  87.0 2.6 collective-permute-start.10
  89.6 0.7 collective-permute-done.2
  90.4 0.5 collective-permute-done.10
  91.0 2.6 collective-permute-start.11
  93.6 0.7 collective-permute-done.3
  94.5 0.5 collective-permute-done.11
  94.9 2.6 collective-permute-start.12
  97.5 0.7 collective-permute-done.4
  98.3 0.5 collective-permute-done.12
  98.9 2.6 collective-permute-start.13
  101.5 0.7 collective-permute-done.5
  102.2 0.6 collective-permute-done.13
  102.8 2.6 collective-permute-start.14
  105.5 0.7 collective-permute-done.6
  106.8 3.3 collective-permute-done.7
  110.1 0.8 concatenate.47
  112.5 0.5 select_reduce_fusion
  113.1 52.7 %pmax.7 = f32[4,284]{1,0:T(4,128)S(1)} all-reduce(f32[4,284]{1,0:T(4,128)S(1)} %constant_dynamic-update-slice_fusion.1), channel_id=1, replica_groups=mesh['req'=2,'seq'=16] {'req','seq'}, use_global_device_ids=true, to_apply=%region_5.6 | all-reduce | flops 1136 | bytes 9088 | tf_op jit(solution)/shard_map/pmax | solution.py:135
  167.0 0.8 copy-done.2
  167.9 0.6 scatter_custom_fusion
  168.4 127.1 %all-reduce.6.cloned.1.call-done = f32[4,284,65]{2,1,0:T(8,128)} async-done(((f32[4,284,65]{2,1,0:T(8,128)}), f32[4,284,65]{2,1,0:T(8,128)}) %all-reduce.6.cloned.1.call-update) | async-done | bytes 295376 | tf_op jit(solution)/shard_map/psum | solution.py:145
  295.5 1.5 slice_reduce_fusion
  297.0 1.3 fusion.1
  299.0 3.4 convolution_add_fusion
  302.5 1.3 dynamic_update_slice.11
  303.9 0.8 copy.77
  304.8 0.8 copy.79
  305.7 125.7 %all-reduce.8.cloned.1.call-done = f32[4,4,4544]{2,0,1:T(4,128)} async-done(((f32[4,4,4544]{2,0,1:T(4,128)}), f32[4,4,4544]{2,0,1:T(4,128)}) %all-reduce.8.cloned.1.call-update) | async-done | bytes 290832 | tf_op jit(solution)/shard_map/psum | solution.py:162
  431.3 1.6 gather_fusion.2
  433.0 0.6 copy.78
  (109 shorter events, 7.9 us)
Async XLA Ops:
  7.2 291.5 %copy-start = (bf16[284,2272]{1,0:T(8,128)(2,1)S(1)}, bf16[284,2272]{1,0:T(8,128)(2,1)}, u32[]{:S(2)}) copy-start(bf16[284,2272]{1,0:T(8,128)(2,1)} %param.19) | copy-start | bytes 3871492
  7.2 70.4 %all-reduce.4.cloned.1.call-start = ((), (), s32[]{:S(2)}) async-start(), calls=%async_computation | async-start | bytes 212992 | tf_op jit(solution)/shard_map/psum | solution.py:73
  51.3 3.5 copy-start.4
  51.3 3.8 copy-start.3
  54.8 1.6 copy-start.8
  54.8 1.7 copy-start.1
  55.1 23.5 %copy-start.5 = (bf16[2,512,128]{2,1,0:T(8,128)(2,1)S(1)}, bf16[2,512,128]{2,1,0:T(8,128)(2,1)}, u32[]{:S(2)}) copy-start(bf16[2,512,128]{2,1,0:T(8,128)(2,1)} %param.12) | copy-start | bytes 786436
  56.3 239.2 %all-reduce.6.cloned.1.call-start = ((), (), s32[]{:S(2)}) async-start(), calls=%async_computation.1 | async-start | bytes 1179648 | tf_op jit(solution)/shard_map/psum | solution.py:145
  77.6 4.1 copy-start.6
  78.4 4.0 collective-permute-start
  79.0 4.0 collective-permute-start.8
  82.4 4.0 collective-permute-start.1
  83.1 4.0 collective-permute-start.9
  86.4 4.0 collective-permute-start.2
  87.0 4.0 collective-permute-start.10
  90.4 4.0 collective-permute-start.3
  91.0 4.0 collective-permute-start.11
  94.3 4.0 collective-permute-start.4
  94.9 4.0 collective-permute-start.12
  98.3 4.0 collective-permute-start.5
  98.9 4.0 collective-permute-start.13
  102.2 4.0 collective-permute-start.6
  102.8 4.0 collective-permute-start.14
  106.2 4.0 collective-permute-start.7
  167.0 0.8 copy-start.2
  167.8 263.5 %all-reduce.8.cloned.1.call-start = ((), (), s32[]{:S(2)}) async-start(), calls=%async_computation.2 | async-start | bytes 589824 | tf_op jit(solution)/shard_map/psum | solution.py:162
  303.8 129.2 %copy-start.7 = (bf16[4,2,284]{2,1,0:T(2,128)(2,1)S(1)}, bf16[4,2,284]{2,1,0:T(2,128)(2,1)}, u32[]{:S(2)}) copy-start(bf16[4,2,284]{2,1,0:T(2,128)(2,1)} %param.11) | copy-start | bytes 13636
Sparse Core Ops, SparseCore 0:
  56.4 21.1 all-reduce.3
  167.9 127.5 all-reduce.5
  304.9 126.4 all-reduce.7
